TPU v7x, 256 devices: a whole 4x4x8 slice. The times are simulated.
256 devices in a mesh: seq: 32 (over x_hi, z, core), tensor: 8 (over y, x_lo).
Axes of the slice: x: 4 (x_hi: 2, x_lo: 2; x = x_hi * 2 + x_lo), y: 4, z: 8, core: 2. Of those that a mesh axis runs over, the one named last changes fastest.
Arguments:
- tokens: bfloat16 [4, 1024, 4096], P(None, 'seq', 'tensor'), may hold values from -600 to 600
- norm_gain: bfloat16 [4096], replicated, may hold values from 0.099609375 to 1.8984375
- w_query: bfloat16 [4096, 2048], P(None, 'tensor'), may hold values from -0.1875 to 0.1875
- w_key: bfloat16 [4096, 2048], P(None, 'tensor'), may hold values from -0.09375 to 0.09375
- w_value: bfloat16 [4096, 2048], P(None, 'tensor'), may hold values from -0.09375 to 0.09375
- w_out: bfloat16 [2048, 4096], P('tensor'), may hold values from -1 to 1
- cache_keys: bfloat16 [4, 8192, 2048], P(None, 'seq', 'tensor'), may hold values from -103 to 103
- cache_values: bfloat16 [4, 8192, 2048], P(None, 'seq', 'tensor'), may hold values from -6 to 6
- cache_len: int32 [4], replicated, may hold values from 1 to 8192, as said below
- group_len: int32 [4], replicated, may hold values from 1 to 1024, 3584 in all
Outputs:
- mixed: bfloat16 [4, 1024, 4096], P(None, 'seq', 'tensor')
- new_keys: bfloat16 [4, 1024, 2048], P(None, 'seq', 'tensor')
- new_values: bfloat16 [4, 1024, 2048], P(None, 'seq', 'tensor')
Inputs may be any that keep to these rules, and one draw needn't show every extreme that they name: `cache_len`: one request's cache holds all 8192 positions. `group_len`: the new-token counts sum to 3584.
All inputs are finite; a program needn't handle non-finite values.
Results may differ from a plain program's by a relative error of at most 0.0075.
The roundings to bfloat16 on the way count: a program that leaves them out, or rounds other values in their place, can miss the bound.
Values may be sent and summed in bfloat16 or wider, within the bound.
No kernel may reach another device: no remote copies, remote signals or barrier semaphores. Data moves between devices by JAX's collectives and lax.ppermute only.
A program may use at most 128 MiB of HBM per device.

v0:
```python
import jax
import jax.numpy as jnp
from jax import lax
from jax.sharding import PartitionSpec as P

HD = 128


def rotate(vector, position):
    half_dim = vector.shape[-1] // 2
    frequency = 1000000.0 ** (-(jnp.arange(half_dim, dtype=jnp.float32) * 2.0 / vector.shape[-1]))
    angles = position.astype(jnp.float32)[..., None] * frequency
    cosine = jnp.concatenate([jnp.cos(angles), jnp.cos(angles)], -1)[..., None, :]
    sine = jnp.concatenate([jnp.sin(angles), jnp.sin(angles)], -1)[..., None, :]
    turned = jnp.concatenate([-vector[..., half_dim:], vector[..., :half_dim]], -1)
    return vector * cosine + turned * sine


def body(
    tokens,
    norm_gain,
    w_query,
    w_key,
    w_value,
    w_out,
    cache_keys,
    cache_values,
    cache_len,
    group_len,
):
    seq_index = lax.axis_index("seq")
    requests, local_rows, width_part = tokens.shape
    gathered = lax.all_gather(tokens, "tensor", axis=2, tiled=True).astype(jnp.float32)
    inverse_rms = lax.rsqrt(jnp.mean(gathered * gathered, -1, keepdims=True) + 1e-05)
    normed = (gathered * inverse_rms * norm_gain.astype(jnp.float32)).astype(jnp.bfloat16)
    flat_rows = normed.reshape(requests * local_rows, -1)
    heads_width = w_query.shape[1]
    local_heads = heads_width // HD

    def project(weight):
        return jnp.dot(flat_rows, weight, preferred_element_type=jnp.float32).reshape(
            requests, local_rows, local_heads, HD
        )

    offsets = jnp.arange(local_rows, dtype=jnp.int32)
    first_row = seq_index * local_rows
    position = cache_len[:, None] + first_row + offsets[None, :]
    queries = (
        rotate(project(w_query), position)
        .astype(jnp.bfloat16)
        .reshape(requests, local_rows, heads_width)
    )
    key_new = (
        rotate(project(w_key), position)
        .astype(jnp.bfloat16)
        .reshape(requests, local_rows, heads_width)
    )
    value_new = project(w_value).astype(jnp.bfloat16).reshape(requests, local_rows, heads_width)
    live_rows = (first_row + offsets)[None, :] < group_len[:, None]
    new_keys = jnp.where(live_rows[..., None], key_new, jnp.zeros_like(key_new))
    new_values = jnp.where(live_rows[..., None], value_new, jnp.zeros_like(value_new))
    all_queries = lax.all_gather(queries, "seq", axis=1, tiled=True)
    group_total = all_queries.shape[1]
    cache_slots = cache_keys.shape[1]
    block_keys = cache_slots + local_rows
    slot_index = seq_index * cache_slots + jnp.arange(cache_slots, dtype=jnp.int32)
    query_index = jnp.arange(group_total, dtype=jnp.int32)
    token_index = first_row + offsets
    score_scale = HD ** (-0.5)
    numer_list = []
    peak_list = []
    mass_list = []
    for request in range(requests):
        query_rows = all_queries[request].reshape(group_total, local_heads, HD)
        key_rows = jnp.concatenate([cache_keys[request], key_new[request]], 0).reshape(
            block_keys, local_heads, HD
        )
        value_rows = jnp.concatenate([cache_values[request], value_new[request]], 0).reshape(
            block_keys, local_heads, HD
        )
        scores = (
            jnp.einsum("qhd,khd->hqk", query_rows, key_rows, preferred_element_type=jnp.float32)
            * score_scale
        )
        cache_ok = slot_index < cache_len[request]
        group_ok = (token_index[None, :] <= query_index[:, None]) & (
            token_index < group_len[request]
        )[None, :]
        usable = jnp.concatenate(
            [jnp.broadcast_to(cache_ok[None, :], (group_total, cache_slots)), group_ok], 1
        )[None]
        row_peak = jnp.max(jnp.where(usable, scores, -1e30), -1)
        weights = jnp.where(usable, jnp.exp(scores - row_peak[..., None]), 0.0)
        row_mass = jnp.sum(weights, -1)
        numer_list.append(
            jnp.einsum(
                "hqk,khd->qhd",
                weights.astype(jnp.bfloat16),
                value_rows,
                preferred_element_type=jnp.float32,
            )
        )
        peak_list.append(row_peak.T)
        mass_list.append(row_mass.T)
    numerators = jnp.stack(numer_list)
    row_peaks = jnp.stack(peak_list)
    row_masses = jnp.stack(mass_list)
    top_peak = lax.pmax(row_peaks.astype(jnp.bfloat16), "seq").astype(row_peaks.dtype)
    factor = jnp.exp(row_peaks - top_peak)
    scaled = (numerators * factor[..., None]).reshape(requests, group_total, heads_width)
    numer_sum, mass_sum = (
        lax.psum_scatter(scaled, "seq", scatter_dimension=1, tiled=True),
        lax.psum_scatter(row_masses * factor, "seq", scatter_dimension=1, tiled=True),
    )
    attended = numer_sum.reshape(requests, local_rows, local_heads, HD) / mass_sum[..., None]
    attended = (
        jnp.where(live_rows[..., None, None], attended, 0.0)
        .astype(jnp.bfloat16)
        .reshape(requests * local_rows, heads_width)
    )
    partial_out = jnp.dot(attended, w_out, preferred_element_type=jnp.float32).reshape(
        requests, local_rows, -1
    )
    mixed = lax.psum_scatter(partial_out, "tensor", scatter_dimension=2, tiled=True).astype(
        jnp.bfloat16
    )
    return (mixed, new_keys, new_values)


def solution(mesh):
    placed = (
        P(None, "seq", "tensor"),
        P(),
        P(None, "tensor"),
        P(None, "tensor"),
        P(None, "tensor"),
        P("tensor", None),
        P(None, "seq", "tensor"),
        P(None, "seq", "tensor"),
        P(),
        P(),
    )
    return jax.shard_map(
        body,
        mesh=mesh,
        in_specs=placed,
        out_specs=(P(None, "seq", "tensor"), P(None, "seq", "tensor"), P(None, "seq", "tensor")),
        check_vma=False,
    )
```

profile of v0, /device:TPU:1, one launch (start us, length us, event | category | flops | bytes accessed | tf_op | source)
XLA Modules:
  0.0 643.1 jit_solution(6151474447986249479)
XLA Ops:
  7.2 0.7 all-gather.3.cloned.1.call-update
  8.0 0.7 convert_element_type.53
  8.7 4.1 copy.101
  12.8 4.1 copy.100
  17.4 34.0 %all-gather.3.cloned.1.call-done = bf16[4,32,4096]{2,1,0:T(8,128)(2,1)} async-done(((bf16[4,32,512]{2,1,0:T(8,128)(2,1)}), bf16[4,32,4096]{2,1,0:T(8,128)(2,1)}) %all-gather.3.cloned.1.call-update) | async-done | bytes 1048592 | tf_op jit(solution)/shard_map/all_gather | solution.py:33
  51.4 1.7 fusion
  53.1 2.8 fusion.77
  55.9 0.8 fusion.79
  57.9 0.7 fusion.106
  58.9 4.1 copy.99
  63.0 0.7 fusion.105
  63.7 1.0 copy.105
  64.7 0.8 copy.60
  66.1 1.2 fusion.84
  67.4 1.0 copy.108
  68.4 0.7 copy.72
  69.1 1.0 copy.107
  70.1 0.8 copy.69
  70.9 1.2 fusion.82
  72.3 0.7 copy.78
  73.1 0.7 copy.75
  74.0 0.8 copy.84
  74.9 0.8 copy.81
  76.3 1.3 broadcast_compare_fusion.1
  77.6 1.4 broadcast_compare_fusion.3
  79.3 0.9 pad_add_fusion.1
  80.2 0.9 pad_add_fusion.2
  81.8 2.8 convolution_convert_fusion
  85.2 57.2 %all-gather.5.cloned.1.call-done = bf16[4,1024,256]{2,1,0:T(8,128)(2,1)} async-done(((bf16[4,32,256]{2,1,0:T(8,128)(2,1)}), bf16[4,1024,256]{2,1,0:T(8,128)(2,1)}) %all-gather.5.cloned.1.call-update) | async-done | bytes 2097168 | tf_op jit(solution)/shard_map/all_gather | solution.py:62
  142.5 2.8 fusion.104
  145.3 1.2 copy.63
  147.2 1.2 fusion.5
  148.4 1.8 fusion.19
  150.2 1.6 copy.86
  151.7 2.1 copy.70
  153.8 1.8 select_reduce_fusion.2
  155.7 1.2 fusion.7
  156.8 1.8 fusion.17
  158.6 2.5 copy.87
  161.2 2.0 copy.76
  163.2 1.9 select_reduce_fusion.1
  165.1 1.2 fusion.9
  166.3 1.8 fusion.15
  168.1 2.6 copy.88
  170.7 2.0 copy.82
  172.7 3.2 select_reduce_fusion
  176.5 124.7 %pmax.7 = bf16[4,1024,2]{1,2,0:T(2,128)(2,1)S(1)} all-reduce(bf16[4,1024,2]{1,2,0:T(2,128)(2,1)} %fusion.103), channel_id=1, replica_groups=mesh['seq'=32,'tensor'=8] {'seq'}, use_global_device_ids=true, to_apply=%region_5.6 | all-reduce | flops 8192 | bytes 32768 | tf_op jit(solution)/shard_map/pmax | solution.py:108
  301.3 2.3 fusion.11
  303.6 0.7 maximum_multiply_fusion.3
  304.2 2.7 copy.90
  307.0 7.0 %mul.122 = f32[4,1024,2,128]{3,2,1,0:T(2,128)} broadcast(f32[4,1024,2]{2,1,0:T(8,128)} %copy.90), dimensions={0,1,2} | broadcast | bytes 4227072 | tf_op jit(solution)/shard_map/mul | solution.py:110
  314.0 6.4 mul.123
  320.4 3.6 fusion.13
  324.0 2.5 copy.89
  326.5 2.4 copy.102
  329.0 3.0 reshape.250
  332.1 5.6 maximum_multiply_fusion
  338.5 105.2 %reduce-scatter.10.cloned.1.call-done = f32[32,8]{1,0:T(8,128)} async-done(((f32[1024,8]{1,0:T(8,128)}), f32[32,8]{1,0:T(8,128)}) %reduce-scatter.10.cloned.1.call-update) | async-done | bytes 1040
  443.7 0.8 reshape.251
  444.8 129.3 %reduce-scatter.6.cloned.1.call-done = f32[4,32,256]{2,1,0:T(8,128)} async-done(((f32[4,1024,256]{2,1,0:T(8,128)}), f32[4,32,256]{2,1,0:T(8,128)}) %reduce-scatter.6.cloned.1.call-update) | async-done | bytes 131088 | tf_op jit(solution)/shard_map/reduce_scatter | solution.py:112
  574.1 2.7 fusion.3
  576.9 0.7 bitcast_select_fusion
  577.6 57.4 %reduce-scatter.8.cloned.1.call-done = f32[4,32,512]{2,1,0:T(8,128)} async-done(((f32[4,32,4096]{2,1,0:T(8,128)}), f32[4,32,512]{2,1,0:T(8,128)}) %reduce-scatter.8.cloned.1.call-update) | async-done | bytes 262160 | tf_op jit(solution)/shard_map/reduce_scatter | solution.py:124
  635.0 1.6 convert_element_type.66
  (92 shorter events, 7.8 us)
Async XLA Ops:
  7.2 567.0 %copy-start = (bf16[256,4096]{1,0:T(8,128)(2,1)S(1)}, bf16[256,4096]{1,0:T(8,128)(2,1)}, u32[]{:S(2)}) copy-start(bf16[256,4096]{1,0:T(8,128)(2,1)} %param.15) | copy-start | bytes 6291460
  7.2 44.2 %all-gather.3.cloned.1.call-start = ((), (), s32[]{:S(2)}) async-start(), calls=%async_computation.3 | async-start | bytes 1179648 | tf_op jit(solution)/shard_map/all_gather | solution.py:33
  7.9 134.6 %all-gather.5.cloned.1.call-start = ((), (), s32[]{:S(2)}) async-start(), calls=%async_computation.4 | async-start | bytes 2162688 | tf_op jit(solution)/shard_map/all_gather | solution.py:62
  12.7 4.2 copy-start.18
  51.4 4.5 copy-start.3
  51.4 4.5 copy-start.4
  53.1 3.7 copy-start.21
  55.9 2.1 copy-start.5
  57.7 386.0 %reduce-scatter.10.cloned.1.call-start = ((), (), s32[]{:S(2)}) async-start(), calls=%async_computation.7 | async-start | bytes 540672
  58.6 4.3 copy-start.6
  63.0 12.7 %copy-start.19 = (s32[4]{0:T(128)S(1)}, s32[4]{0:T(128)}, u32[]{:S(2)}) copy-start(s32[4]{0:T(128)} %param.19) | copy-start | bytes 52
  67.4 14.5 %copy-start.22 = (f32[4,32]{1,0:T(4,128)S(1)}, f32[4,32]{1,0:T(4,128)}, u32[]{:S(2)}) copy-start(f32[4,32]{1,0:T(4,128)} %copy-done.21) | copy-start | bytes 1540
  75.6 9.0 %copy-start.23 = (s32[32]{0:T(128)}, s32[32]{0:T(128)S(1)}, u32[]{:S(2)}) copy-start(s32[32]{0:T(128)S(1)} %iota_add_fusion.1) | copy-start | bytes 388
  84.6 62.0 %copy-start.7 = (bf16[4,32,2,128]{3,1,2,0:T(8,128)(2,1)}, bf16[4,32,2,128]{3,1,2,0:T(8,128)(2,1)S(1)}, u32[]{:S(2)}) copy-start(bf16[4,32,2,128]{3,1,2,0:T(8,128)(2,1)S(1)} %convolution_convert_fusion) | copy-start | bytes 196612
  146.6 1.8 copy-start.9
  153.8 1.9 copy-start.2
  153.8 3.0 copy-start.10
  153.8 3.0 copy-start.17
  163.2 1.9 copy-start.1
  163.2 3.0 copy-start.11
  163.2 3.0 copy-start.16
  301.3 2.3 copy-start.12
  301.3 2.3 copy-start.13
  301.3 2.3 copy-start.14
  314.0 6.4 copy-start.15
  332.0 242.1 %reduce-scatter.6.cloned.1.call-start = ((), (), s32[]{:S(2)}) async-start(), calls=%async_computation.5 | async-start | bytes 4325376 | tf_op jit(solution)/shard_map/reduce_scatter | solution.py:112
  337.7 0.7 copy-start.20
  337.7 0.7 copy-start.24
  337.8 297.2 %reduce-scatter.8.cloned.1.call-start = ((), (), s32[]{:S(2)}) async-start(), calls=%async_computation.6 | async-start | bytes 2359296 | tf_op jit(solution)/shard_map/reduce_scatter | solution.py:124
  444.8 132.0 %copy-start.8 = (bf16[4,32,2,128]{3,1,2,0:T(8,128)(2,1)S(1)}, bf16[4,32,2,128]{3,1,2,0:T(8,128)(2,1)}, u32[]{:S(2)}) copy-start(bf16[4,32,2,128]{3,1,2,0:T(8,128)(2,1)} %copy-done.7) | copy-start | bytes 196612
Sparse Core Ops, SparseCore 0:
  9.8 41.5 all-gather.2
  57.8 84.5 all-gather.4
  332.2 111.4 reduce-scatter.9
  447.8 126.3 reduce-scatter.5
  577.0 57.9 reduce-scatter.7
where the time goes:
time: 645 us; the launch traced here: 643 us
  waiting for transfers between devices  384 us (60%)
  blocking collectives  125 us (19%)
  local copies, waits for them, and re-layouts  68.8 us (11%)
  matrix products  25.7 us (4%)
  other arithmetic  25.6 us (4%)
  between operations  14.2 us (2%)
    reduce_scatter x1, waiting for transfers between devices, body(): lax.psum_scatter(scaled, 'seq', scatter_dimension=1, tiled=True)  129 us
    pmax x1, blocking collectives, body(): lax.pmax(row_peaks.astype(jnp.bfloat16), 'seq').astype(row_peaks.dtype)  125 us
    unnamed x6, waiting for transfers between devices  106 us
    reduce_scatter x1, waiting for transfers between devices, body(): lax.psum_scatter(partial_out, 'tensor', scatter_dimension=2, tiled=True)  57.4 us
    all_gather x1, waiting for transfers between devices, body(): all_queries = lax.all_gather(queries, 'seq', axis=1, tiled=True)  57.2 us
    all_gather x1, waiting for transfers between devices, body(): lax.all_gather(tokens, 'tensor', axis=2, tiled=True).astype(jnp.float32)  34 us
    mul x2, local copies, waits for them, and re-layouts, body(): numerators * factor[..., None]  13.4 us
  transfers between devices with their start and end apart: 5, of which 5 were waited for; matrix products, arithmetic and copies ran while one was open for 7% of the time, Pallas kernels for 0%

commit v1 on v0

--- a/solution.py
+++ b/solution.py
@@ -30,7 +30,9 @@
 ):
     seq_index = lax.axis_index("seq")
     requests, local_rows, width_part = tokens.shape
-    gathered = lax.all_gather(tokens, "tensor", axis=2, tiled=True).astype(jnp.float32)
+    gathered = jnp.concatenate(
+        lax.all_to_all(jnp.stack([tokens] * lax.axis_size("tensor")), "tensor", 0, 0), axis=2
+    ).astype(jnp.float32)
     inverse_rms = lax.rsqrt(jnp.mean(gathered * gathered, -1, keepdims=True) + 1e-05)
     normed = (gathered * inverse_rms * norm_gain.astype(jnp.float32)).astype(jnp.bfloat16)
     flat_rows = normed.reshape(requests * local_rows, -1)

time: 645 us -> 614 us (0.952)
  waiting for transfers between devices: 384 us -> 352 us
    all_gather x1 -> x0, waiting for transfers between devices: 34 us -> none  [body(): lax.all_gather(tokens, 'tensor', axis=2, tiled=True).astype(jnp.float32)]
    unnamed x6 -> x5, waiting for transfers between devices: 106 us -> 105 us
where the time goes in v1:
time: 614 us; the launch traced here: 613 us
  waiting for transfers between devices  352 us (57%)
  blocking collectives  125 us (20%)
  local copies, waits for them, and re-layouts  71.7 us (12%)
  matrix products  22.5 us (4%)
  other arithmetic  22.3 us (4%)
  between operations  14.2 us (2%)
    reduce_scatter x1, waiting for transfers between devices, body(): lax.psum_scatter(scaled, 'seq', scatter_dimension=1, tiled=True)  129 us
    pmax x1, blocking collectives, body(): lax.pmax(row_peaks.astype(jnp.bfloat16), 'seq').astype(row_peaks.dtype)  125 us
    unnamed x5, waiting for transfers between devices  105 us
    reduce_scatter x1, waiting for transfers between devices, body(): lax.psum_scatter(partial_out, 'tensor', scatter_dimension=2, tiled=True)  57.3 us
    all_gather x1, waiting for transfers between devices, body(): all_queries = lax.all_gather(queries, 'seq', axis=1, tiled=True)  54.7 us
    mul x2, local copies, waits for them, and re-layouts, body(): numerators * factor[..., None]  13.4 us
    dot_general x3, local copies, waits for them, and re-layouts, project(): jnp.dot(flat_rows, weight, preferred_element_type=jnp.float32)  12.4 us
  transfers between devices with their start and end apart: 5, of which 5 were waited for; matrix products, arithmetic and copies ran while one was open for 7% of the time, Pallas kernels for 0%

profile of v1, /device:TPU:1, one launch (start us, length us, event | category | flops | bytes accessed | tf_op | source)
XLA Modules:
  0.0 613.2 jit_solution(8695356726368112036)
XLA Ops:
  7.2 2.2 stack.56
  9.3 5.9 all-to-all-start
  15.4 4.1 copy.138
  19.5 4.1 copy.137
  24.1 5.7 all-to-all-done
  31.1 1.3 reshape.301
  32.4 2.9 fusion.38
  35.3 0.8 fusion.40
  37.2 0.7 fusion.106
  38.1 4.1 copy.136
  42.2 0.7 fusion.105
  43.0 1.0 copy.142
  44.0 0.8 copy.97
  45.4 1.3 fusion.84
  46.8 1.0 copy.145
  47.8 0.8 copy.109
  48.6 1.0 copy.144
  49.6 0.8 copy.106
  50.3 1.2 fusion.82
  51.7 0.8 copy.115
  52.5 0.8 copy.112
  53.4 0.8 copy.121
  54.3 0.7 copy.118
  55.7 1.3 broadcast_compare_fusion.1
  57.0 1.3 broadcast_compare_fusion.3
  58.6 0.9 pad_add_fusion.1
  59.4 0.9 pad_add_fusion.2
  61.1 2.8 convolution_convert_fusion
  64.5 54.7 %all-gather.2.cloned.1.call-done = bf16[4,1024,256]{2,1,0:T(8,128)(2,1)} async-done(((bf16[4,32,256]{2,1,0:T(8,128)(2,1)}), bf16[4,1024,256]{2,1,0:T(8,128)(2,1)}) %all-gather.2.cloned.1.call-update) | async-done | bytes 2097168 | tf_op jit(solution)/shard_map/all_gather | solution.py:64
  119.2 2.8 fusion.104
  122.1 1.2 copy.100
  124.0 1.2 fusion.5
  125.1 1.8 fusion.19
  127.0 1.6 copy.123
  128.5 2.1 copy.107
  130.6 1.8 select_reduce_fusion.2
  132.4 1.1 fusion.7
  133.6 1.8 fusion.17
  135.4 2.6 copy.124
  138.0 2.1 copy.113
  140.1 1.9 select_reduce_fusion.1
  142.0 1.2 fusion.9
  143.1 1.8 fusion.15
  144.9 2.6 copy.125
  147.5 2.1 copy.119
  149.5 1.8 select_reduce_fusion
  151.3 1.2 fusion.11
  152.5 1.8 fusion.13
  154.3 2.7 copy.126
  157.1 124.5 %pmax.7 = bf16[4,1024,2]{1,2,0:T(2,128)(2,1)S(1)} all-reduce(bf16[4,1024,2]{1,2,0:T(2,128)(2,1)S(1)} %fusion.103), channel_id=1, replica_groups=mesh['seq'=32,'tensor'=8] {'seq'}, use_global_device_ids=true, to_apply=%region_5.6 | all-reduce | flops 8192 | bytes 32768 | tf_op jit(solution)/shard_map/pmax | solution.py:110
  281.6 0.8 maximum_multiply_fusion.3
  282.4 2.0 copy.127
  284.4 7.0 %mul.158 = f32[4,1024,2,128]{3,2,1,0:T(2,128)} broadcast(f32[4,1024,2]{2,1,0:T(8,128)} %copy.127), dimensions={0,1,2} | broadcast | bytes 4227072 | tf_op jit(solution)/shard_map/mul | solution.py:112
  291.4 6.4 %mul.159 = f32[4,1024,256]{2,1,0:T(8,128)} reshape(f32[4,1024,2,128]{3,2,1,0:T(2,128)} %mul.158) | data formatting | bytes 8388608 | tf_op jit(solution)/shard_map/mul | solution.py:112
  297.8 1.7 copy.139
  299.5 3.0 reshape.307
  302.6 5.6 maximum_multiply_fusion
  309.0 104.6 %reduce-scatter.10.cloned.1.call-done = f32[32,8]{1,0:T(8,128)} async-done(((f32[1024,8]{1,0:T(8,128)}), f32[32,8]{1,0:T(8,128)}) %reduce-scatter.10.cloned.1.call-update) | async-done | bytes 1040
  413.6 0.8 reshape.308
  414.8 129.5 %reduce-scatter.6.cloned.1.call-done = f32[4,32,256]{2,1,0:T(8,128)} async-done(((f32[4,1024,256]{2,1,0:T(8,128)}), f32[4,32,256]{2,1,0:T(8,128)}) %reduce-scatter.6.cloned.1.call-update) | async-done | bytes 131088 | tf_op jit(solution)/shard_map/reduce_scatter | solution.py:114
  544.3 2.7 fusion.3
  547.1 0.7 bitcast_select_fusion
  547.8 57.3 %reduce-scatter.8.cloned.1.call-done = f32[4,32,512]{2,1,0:T(8,128)} async-done(((f32[4,32,4096]{2,1,0:T(8,128)}), f32[4,32,512]{2,1,0:T(8,128)}) %reduce-scatter.8.cloned.1.call-update) | async-done | bytes 262160 | tf_op jit(solution)/shard_map/reduce_scatter | solution.py:126
  605.1 1.6 convert_element_type.98
  (93 shorter events, 8.2 us)
Async XLA Ops:
  7.2 537.1 %copy-start = (bf16[256,4096]{1,0:T(8,128)(2,1)S(1)}, bf16[256,4096]{1,0:T(8,128)(2,1)}, u32[]{:S(2)}) copy-start(bf16[256,4096]{1,0:T(8,128)(2,1)} %param.15) | copy-start | bytes 6291460
  7.2 8.1 %copy-start.18 = (bf16[4096]{0:T(1024)(128)(2,1)S(1)}, bf16[4096]{0:T(1024)(128)(2,1)}, u32[]{:S(2)}) copy-start(bf16[4096]{0:T(1024)(128)(2,1)} %param.11) | copy-start | bytes 24580
  9.3 20.5 %all-to-all-start = ((bf16[8,4,32,512]{3,2,1,0:T(8,128)(2,1)}), bf16[8,4,32,512]{3,2,1,0:T(8,128)(2,1)S(1)}, u32[]{:S(2)}, u32[]{:S(2)}) async-start(bf16[8,4,32,512]{3,2,1,0:T(8,128)(2,1)} %stack.56), calls=%async_computation | async-start | bytes 2097152 | tf_op jit(solution)/shard_map/all_to_all | solution.py:34
  15.3 103.9 %all-gather.2.cloned.1.call-start = ((), (), s32[]{:S(2)}) async-start(), calls=%async_computation.4 | async-start | bytes 2162688 | tf_op jit(solution)/shard_map/all_gather | solution.py:64
  19.5 4.1 copy-start.19
  32.4 2.9 copy-start.3
  32.4 2.9 copy-start.4
  35.3 1.9 copy-start.5
  37.1 376.5 %reduce-scatter.10.cloned.1.call-start = ((), (), s32[]{:S(2)}) async-start(), calls=%async_computation.7 | async-start | bytes 540672
  37.9 4.4 copy-start.6
  42.2 12.8 %copy-start.20 = (s32[4]{0:T(128)S(1)}, s32[4]{0:T(128)}, u32[]{:S(2)}) copy-start(s32[4]{0:T(128)} %param.19) | copy-start | bytes 52
  55.0 8.8 %copy-start.22 = (s32[32]{0:T(128)}, s32[32]{0:T(128)S(1)}, u32[]{:S(2)}) copy-start(s32[32]{0:T(128)S(1)} %iota_add_fusion.1) | copy-start | bytes 388
  63.8 59.5 %copy-start.7 = (bf16[4,32,2,128]{3,1,2,0:T(8,128)(2,1)}, bf16[4,32,2,128]{3,1,2,0:T(8,128)(2,1)S(1)}, u32[]{:S(2)}) copy-start(bf16[4,32,2,128]{3,1,2,0:T(8,128)(2,1)S(1)} %convolution_convert_fusion) | copy-start | bytes 196612
  123.3 1.8 copy-start.9
  130.6 1.9 copy-start.2
  130.6 3.0 copy-start.11
  130.6 3.0 copy-start.17
  140.1 1.9 copy-start.1
  140.1 3.0 copy-start.12
  140.1 3.0 copy-start.16
  149.5 3.0 copy-start.10
  149.5 3.0 copy-start.15
  152.5 129.1 %copy-start.13 = (f32[2,1024]{1,0:T(2,128)S(1)}, f32[2,1024]{1,0:T(2,128)}, u32[]{:S(2)}) copy-start(f32[2,1024]{1,0:T(2,128)} %fusion.5) | copy-start | bytes 24580
  152.5 129.1 %copy-start.14 = (f32[2,1024]{1,0:T(2,128)S(1)}, f32[2,1024]{1,0:T(2,128)}, u32[]{:S(2)}) copy-start(f32[2,1024]{1,0:T(2,128)} %fusion.7) | copy-start | bytes 24580
  302.6 241.7 %reduce-scatter.6.cloned.1.call-start = ((), (), s32[]{:S(2)}) async-start(), calls=%async_computation.5 | async-start | bytes 4325376 | tf_op jit(solution)/shard_map/reduce_scatter | solution.py:114
  308.3 0.7 copy-start.21
  308.3 0.7 copy-start.23
  308.3 296.8 %reduce-scatter.8.cloned.1.call-start = ((), (), s32[]{:S(2)}) async-start(), calls=%async_computation.6 | async-start | bytes 2359296 | tf_op jit(solution)/shard_map/reduce_scatter | solution.py:126
  414.8 132.3 %copy-start.8 = (bf16[4,32,2,128]{3,1,2,0:T(8,128)(2,1)S(1)}, bf16[4,32,2,128]{3,1,2,0:T(8,128)(2,1)}, u32[]{:S(2)}) copy-start(bf16[4,32,2,128]{3,1,2,0:T(8,128)(2,1)} %copy-done.7) | copy-start | bytes 196612
Sparse Core Ops, SparseCore 0:
  37.2 81.9 all-gather.1
  302.7 110.8 reduce-scatter.9
  417.9 126.3 reduce-scatter.5
  547.2 57.8 reduce-scatter.7
